TPU v7x, 512 devices: a whole 4x4x16 slice. The times are simulated.
512 devices in a mesh: seq: 64 (over z, y), tp: 4 (over x), dp: 2 (over core).
Axes of the slice: x: 4, y: 4, z: 16, core: 2. Of those that a mesh axis runs over, the one named last changes fastest.
Arguments:
- inputs: bfloat16 [16384, 1280], P(('dp', 'seq'), 'tp'), parts along dimension 0, may hold values from -6 to 6
- out_grads: bfloat16 [16384, 1280], P(('dp', 'seq'), 'tp'), parts along dimension 0, may hold values from -6 to 6
- norm_gain: float32 [1280], replicated, may hold values from 0.1 to 1.9
- w_query: bfloat16 [640, 1280], P('tp'), may hold values from -0.15625 to 0.15625
- w_key: bfloat16 [640, 1280], P('tp'), may hold values from -0.15625 to 0.15625
- w_value: bfloat16 [640, 1280], P('tp'), may hold values from -0.15625 to 0.15625
- w_output: bfloat16 [640, 1280], P('tp'), may hold values from -0.25 to 0.25
- query_scale: float32 [80], replicated, may hold values from -4 to 4
- offsets: int32 [64], replicated, may hold values from 0 to 63, each once
Outputs:
- input_grads: bfloat16 [16384, 1280], P(('dp', 'seq'), 'tp'), parts along dimension 0
There are 2 independent parts, one for each index of `dp`. A program takes and returns all parts, laid end to end along the dimension named above; an argument that names none is the same for every part. Nothing has to cross between parts.
Inputs may be any that keep to these rules, and one draw needn't show every extreme that they name: `offsets`: each number appears exactly once.
All inputs are finite; a program needn't handle non-finite values.
Results may differ from a plain program's by a relative error of at most 0.007.
The roundings to bfloat16 on the way count: a program that leaves them out, or rounds other values in their place, can miss the bound.
Values may be sent and summed in bfloat16 or wider, within the bound.
No kernel may reach another device: no remote copies, remote signals or barrier semaphores. Data moves between devices by JAX's collectives and lax.ppermute only.
A program may use at most 64 MiB of HBM per device.

v0:
```python
import math
import jax
import jax.numpy as jnp
import numpy as np
from jax import lax
from jax.sharding import Mesh
from jax.sharding import PartitionSpec as P

PIECE = 128
scale_base = 1.4426950408889634
masked_score = -1e30
norm_eps = 1e-06


def column_scale(query_scale, head_count):
    head_width = query_scale.shape[0]
    factor = scale_base / math.sqrt(head_width) * jax.nn.softplus(query_scale)
    return jnp.tile(factor, head_count)


def block_positions(offsets, rows):
    return (offsets[:, None] * PIECE + lax.iota(jnp.int32, PIECE)[None, :]).reshape(rows)


def ring_steps(size):
    return (size // 2, (size - 1) // 2)


def shift(data, axis, size, step):
    return lax.ppermute(data, axis, [(i, (i + step) % size) for i in range(size)])


def ring_gather(data, axis, size):
    forward, backward = ring_steps(size)
    pieces = [None] * size
    pieces[0] = data
    ahead = behind = data
    for step in range(max(forward, backward)):
        if step < forward:
            ahead = shift(ahead, axis, size, 1)
            pieces[size - 1 - step] = ahead
        if step < backward:
            behind = shift(behind, axis, size, -1)
            pieces[1 + step] = behind
    return pieces


def ring4_first(data, axis):
    return (shift(data, axis, 4, 1), shift(data, axis, 4, -1))


def ring4_last(data, ahead, behind, axis):
    half = data.shape[0] // 2
    far = jnp.concatenate(
        [shift(ahead[:half], axis, 4, 1), shift(behind[half:], axis, 4, -1)], axis=0
    )
    return [data, behind, far, ahead]


def per_device(
    inputs, out_grads, norm_gain, w_query, w_key, w_value, w_output, query_scale, offsets
):
    row_count, width_here = inputs.shape
    head_width = query_scale.shape[0]
    heads_here = w_query.shape[0] // head_width
    cols = heads_here * head_width
    tp_size = lax.axis_size("tp")
    y_size = lax.axis_size("y")
    shards = offsets.shape[0]
    all_rows = shards * row_count
    contract = (((1,), (1,)), ((), ()))
    with jax.named_scope("gather_features"):
        both = jnp.concatenate([inputs, out_grads], axis=1)
        gathered = lax.all_gather(both, "tp", axis=1, tiled=True)
        gathered = gathered.reshape(row_count, tp_size, 2, width_here)
        full_inputs = gathered[:, :, 0, :].reshape(row_count, tp_size * width_here)
        full_grads = gathered[:, :, 1, :].reshape(row_count, tp_size * width_here)
    full_width = full_inputs.shape[1]
    with jax.named_scope("projections"):
        widened = full_inputs.astype(jnp.float32)
        inverse = lax.rsqrt(jnp.mean(widened * widened, axis=1, keepdims=True) + norm_eps)
        normed = (widened * inverse * norm_gain[None, :]).astype(jnp.bfloat16)
        factor = column_scale(query_scale, heads_here)
        queries = (
            lax.dot_general(normed, w_query, contract, preferred_element_type=jnp.float32)
            * factor[None, :]
        ).astype(jnp.bfloat16)
        keys = lax.dot_general(normed, w_key, contract, preferred_element_type=jnp.float32).astype(
            jnp.bfloat16
        )
        values = lax.dot_general(
            normed, w_value, contract, preferred_element_type=jnp.float32
        ).astype(jnp.bfloat16)
        head_grads = lax.dot_general(
            full_grads, w_output, contract, preferred_element_type=jnp.float32
        ).astype(jnp.bfloat16)
    z_size = lax.axis_size("z")
    z_index = lax.axis_index("z")
    y_index = lax.axis_index("y")
    with jax.named_scope("gather_sequence"):
        kv = jnp.concatenate([keys, values], axis=1)
        qg = jnp.concatenate([queries, head_grads], axis=1)
        kv_all = lax.all_gather(kv, "y", axis=0, tiled=True)
        kv_all = lax.all_gather(kv_all, "z", axis=0, tiled=True)
        qg_z = jnp.concatenate(ring_gather(qg, "z", z_size), axis=0)
        qg_ahead, qg_behind = ring4_first(qg_z, "y")
        key_all = kv_all[:, :cols].reshape(all_rows, heads_here, head_width)
        value_all = kv_all[:, cols:].reshape(all_rows, heads_here, head_width)
    rel_z = lax.iota(jnp.int32, z_size)
    rel_y = lax.iota(jnp.int32, y_size)
    abs_z = (z_index + rel_z) % z_size
    abs_y = (y_index + rel_y) % y_size
    qg_source = (abs_z[None, :] * y_size + abs_y[:, None]).reshape(shards)
    key_positions = block_positions(offsets, all_rows)
    seq_index = z_index * y_size + y_index
    own_positions = offsets[seq_index] * PIECE + lax.iota(jnp.int32, row_count)
    query_heads = queries.reshape(row_count, heads_here, head_width)
    grad_heads = head_grads.reshape(row_count, heads_here, head_width)
    key_heads = keys.reshape(row_count, heads_here, head_width)
    value_heads = values.reshape(row_count, heads_here, head_width)
    with jax.named_scope("query_pass"):
        scores = jnp.einsum(
            "qhd,khd->hqk", query_heads, key_all, preferred_element_type=jnp.float32
        )
        visible = key_positions[None, None, :] <= own_positions[None, :, None]
        masked = jnp.where(visible, scores, masked_score)
        row_peak = jnp.max(masked, axis=2)
        summed = jnp.sum(jnp.where(visible, jnp.exp(masked - row_peak[:, :, None]), 0.0), axis=2)
        log_total = row_peak + jnp.log(summed)
        attend = jnp.exp(jnp.where(visible, scores - log_total[:, :, None], masked_score))
        grad_probs = jnp.einsum(
            "qhd,khd->hqk", grad_heads, value_all, preferred_element_type=jnp.float32
        )
        weighted = attend * grad_probs
        row_delta = jnp.sum(weighted, axis=2)
        first_sum = jnp.einsum(
            "hqk,khd->hqd",
            weighted.astype(jnp.bfloat16),
            key_all,
            preferred_element_type=jnp.float32,
        )
        second_sum = jnp.einsum(
            "hqk,khd->hqd", attend.astype(jnp.bfloat16), key_all, preferred_element_type=jnp.float32
        )
        query_grad = first_sum - row_delta[:, :, None] * second_sum
        query_grad = jnp.transpose(query_grad, (1, 0, 2)).reshape(row_count, cols)
        query_done = (query_grad * factor[None, :]).astype(jnp.bfloat16)
    with jax.named_scope("gather_row_stats"):
        stats = jnp.stack([log_total, row_delta], axis=0)
        stats, qg_ahead, qg_behind = lax.optimization_barrier((stats, qg_ahead, qg_behind))
        qg_pieces = ring4_last(qg_z, qg_ahead, qg_behind, "y")
        sent = jnp.broadcast_to(stats[None], (shards,) + stats.shape)
        stats_all = lax.all_to_all(sent, ("z", "y"), 0, 0, tiled=False)
    with jax.named_scope("key_pass"):
        piece_rows = qg_pieces[0].shape[0]
        stats_ordered = stats_all[qg_source]
        query_places = block_positions(offsets[qg_source], all_rows)
        key_grad = jnp.zeros((row_count, heads_here, head_width), jnp.float32)
        value_grad = jnp.zeros((row_count, heads_here, head_width), jnp.float32)
        for ry, piece in enumerate(qg_pieces):
            source = qg_source[ry * z_size : (ry + 1) * z_size]
            query_part = piece[:, :cols].reshape(piece_rows, heads_here, head_width)
            grad_part = piece[:, cols:].reshape(piece_rows, heads_here, head_width)
            place = query_places[ry * piece_rows : (ry + 1) * piece_rows]
            part_stats = stats_ordered[ry * z_size : (ry + 1) * z_size]
            log_part = jnp.transpose(part_stats[:, 0], (1, 0, 2)).reshape(heads_here, piece_rows)
            delta_part = jnp.transpose(part_stats[:, 1], (1, 0, 2)).reshape(heads_here, piece_rows)
            scores_t = jnp.einsum(
                "khd,qhd->hkq", key_heads, query_part, preferred_element_type=jnp.float32
            )
            visible_t = own_positions[None, :, None] <= place[None, None, :]
            attend_t = jnp.exp(jnp.where(visible_t, scores_t - log_part[:, None, :], masked_score))
            grad_probs_t = jnp.einsum(
                "khd,qhd->hkq", value_heads, grad_part, preferred_element_type=jnp.float32
            )
            score_grad = (attend_t * (grad_probs_t - delta_part[:, None, :])).astype(jnp.bfloat16)
            plain_t = attend_t.astype(jnp.bfloat16)
            score_grad, plain_t = lax.optimization_barrier((score_grad, plain_t))
            key_grad = key_grad + jnp.einsum(
                "hkq,qhd->khd", score_grad, query_part, preferred_element_type=jnp.float32
            )
            value_grad = value_grad + jnp.einsum(
                "hkq,qhd->khd", plain_t, grad_part, preferred_element_type=jnp.float32
            )
        key_done = key_grad.reshape(row_count, cols).astype(jnp.bfloat16)
        value_done = value_grad.reshape(row_count, cols).astype(jnp.bfloat16)
    with jax.named_scope("back_projection"):
        back_sum = jnp.dot(query_done, w_query, preferred_element_type=jnp.float32)
        back_sum = back_sum + jnp.dot(key_done, w_key, preferred_element_type=jnp.float32)
        back_sum = back_sum + jnp.dot(value_done, w_value, preferred_element_type=jnp.float32)
        scaled = back_sum * norm_gain[None, :]
        row_part = jnp.sum(widened * scaled, axis=1)
        chunks = scaled.reshape(row_count, tp_size, width_here).transpose(1, 0, 2)
        extra = jnp.zeros((tp_size, 1, width_here), jnp.float32)
        extra = extra.at[:, 0, :row_count].set(jnp.broadcast_to(row_part, (tp_size, row_count)))
        payload = jnp.concatenate([chunks, extra], axis=1)
        received = lax.all_to_all(payload, "tp", 0, 0, tiled=False)
        total = jnp.sum(received, axis=0)
        scaled_own = total[:row_count]
        row_dot = total[row_count, :row_count][:, None]
    with jax.named_scope("input_grads"):
        start_col = lax.axis_index("tp") * width_here
        own_inputs = inputs.astype(jnp.float32)
        branch = (
            inverse * scaled_own - own_inputs * inverse * inverse * inverse * row_dot / full_width
        )
        result = out_grads.astype(jnp.float32) + branch
    return result.astype(jnp.bfloat16)


def solution(mesh):
    seq_size = mesh.shape["seq"]
    devices = mesh.devices
    y_size = 4 if seq_size % 4 == 0 else 1
    split = Mesh(
        devices.reshape((seq_size // y_size, y_size) + devices.shape[1:]), ("z", "y", "tp", "dp")
    )
    rows = P(("dp", "z", "y"), "tp")
    return jax.shard_map(
        per_device,
        mesh=split,
        in_specs=(
            rows,
            rows,
            P(),
            P("tp", None),
            P("tp", None),
            P("tp", None),
            P("tp", None),
            P(),
            P(),
        ),
        out_specs=rows,
        check_vma=False,
    )
```

profile of v0, /device:TPU:2, one launch (start us, length us, event | category | flops | bytes accessed | tf_op | source)
XLA Modules:
  0.0 219.6 jit_solution(6411096085846394718)
XLA Ops:
  7.5 15.7 %all_gather.9 = bf16[128,2560]{0,1:T(8,128)(2,1)S(1)} all-gather(bf16[128,640]{0,1:T(8,128)(2,1)S(1)} %pad_maximum_fusion.1), channel_id=1, replica_groups=mesh['z'=16,'y'=4,'tp'=4,'dp'=2] {'tp'}, dimensions={1}, use_global_device_ids=true | all-gather | bytes 819200 | tf_op jit(solution)/shard_map/gather_features/all_gather | solution.py:74
  24.7 12.3 %all_gather.10 = bf16[512,320]{0,1:T(8,128)(2,1)} all-gather(bf16[128,320]{0,1:T(8,128)(2,1)S(1)} %pad_maximum_fusion.2), channel_id=1, replica_groups=mesh['z'=16,'y'=4,'tp'=4,'dp'=2] {'y'}, dimensions={0}, use_global_device_ids=true | all-gather | bytes 409600 | tf_op jit(solution)/shard_map/gather_sequence/all_gather | solution.py:103
  38.4 10.8 %collective-permute-start = (bf16[128,320]{0,1:T(8,128)(2,1)S(1)}, bf16[128,320]{0,1:T(8,128)(2,1)S(1)}, u32[]{:S(2)}, u32[]{:S(2)}) collective-permute-start(bf16[128,320]{0,1:T(8,128)(2,1)S(1)} %get-tuple-element.59), channel_id=1, source_target_pairs={{0,480},{32,0},{64,32},{96,64},{128,96},{160,128},{192,160},{224,1... | collective-permute-start | bytes 245768 | tf_op jit(solution)/shard_map/gather_sequence/ppermute | solution.py:30
  49.1 1.9 collective-permute-start.7
  55.8 5.1 %collective-permute-start.1 = (bf16[128,320]{0,1:T(8,128)(2,1)S(1)}, bf16[128,320]{0,1:T(8,128)(2,1)S(1)}, u32[]{:S(2)}, u32[]{:S(2)}) collective-permute-start(bf16[128,320]{0,1:T(8,128)(2,1)S(1)} %collective-permute-done), channel_id=1, source_target_pairs={{0,480},{32,0},{64,32},{96,64},{128,96},{160,128},{192,160},{224,1... | collective-permute-start | bytes 245768 | tf_op jit(solution)/shard_map/gather_sequence/ppermute | solution.py:30
  60.9 1.9 collective-permute-start.8
  64.5 5.6 %collective-permute-start.2 = (bf16[128,320]{0,1:T(8,128)(2,1)S(1)}, bf16[128,320]{0,1:T(8,128)(2,1)S(1)}, u32[]{:S(2)}, u32[]{:S(2)}) collective-permute-start(bf16[128,320]{0,1:T(8,128)(2,1)S(1)} %collective-permute-done.1), channel_id=1, source_target_pairs={{0,480},{32,0},{64,32},{96,64},{128,96},{160,128},{192,160},{224,1... | collective-permute-start | bytes 245768 | tf_op jit(solution)/shard_map/gather_sequence/ppermute | solution.py:30
  70.5 1.9 collective-permute-start.9
  73.3 5.6 %collective-permute-start.3 = (bf16[128,320]{0,1:T(8,128)(2,1)S(1)}, bf16[128,320]{0,1:T(8,128)(2,1)S(1)}, u32[]{:S(2)}, u32[]{:S(2)}) collective-permute-start(bf16[128,320]{0,1:T(8,128)(2,1)S(1)} %collective-permute-done.2), channel_id=1, source_target_pairs={{0,480},{32,0},{64,32},{96,64},{128,96},{160,128},{192,160},{224,1... | collective-permute-start | bytes 245768 | tf_op jit(solution)/shard_map/gather_sequence/ppermute | solution.py:30
  79.7 1.9 collective-permute-start.10
  82.7 5.6 %collective-permute-start.4 = (bf16[128,320]{0,1:T(8,128)(2,1)S(1)}, bf16[128,320]{0,1:T(8,128)(2,1)S(1)}, u32[]{:S(2)}, u32[]{:S(2)}) collective-permute-start(bf16[128,320]{0,1:T(8,128)(2,1)S(1)} %collective-permute-done.3), channel_id=1, source_target_pairs={{0,480},{32,0},{64,32},{96,64},{128,96},{160,128},{192,160},{224,1... | collective-permute-start | bytes 245768 | tf_op jit(solution)/shard_map/gather_sequence/ppermute | solution.py:30
  88.9 1.9 collective-permute-start.11
  91.5 5.6 %collective-permute-start.5 = (bf16[128,320]{0,1:T(8,128)(2,1)S(1)}, bf16[128,320]{0,1:T(8,128)(2,1)S(1)}, u32[]{:S(2)}, u32[]{:S(2)}) collective-permute-start(bf16[128,320]{0,1:T(8,128)(2,1)S(1)} %collective-permute-done.4), channel_id=1, source_target_pairs={{0,480},{32,0},{64,32},{96,64},{128,96},{160,128},{192,160},{224,1... | collective-permute-start | bytes 245768 | tf_op jit(solution)/shard_map/gather_sequence/ppermute | solution.py:30
  100.4 5.6 %collective-permute-start.6 = (bf16[128,320]{0,1:T(8,128)(2,1)S(1)}, bf16[128,320]{0,1:T(8,128)(2,1)S(1)}, u32[]{:S(2)}, u32[]{:S(2)}) collective-permute-start(bf16[128,320]{0,1:T(8,128)(2,1)S(1)} %collective-permute-done.5), channel_id=1, source_target_pairs={{0,480},{32,0},{64,32},{96,64},{128,96},{160,128},{192,160},{224,1... | collective-permute-start | bytes 245768 | tf_op jit(solution)/shard_map/gather_sequence/ppermute | solution.py:30
  109.3 6.3 %collective-permute-done.13 = bf16[128,320]{0,1:T(8,128)(2,1)S(1)} collective-permute-done((bf16[128,320]{0,1:T(8,128)(2,1)S(1)}, bf16[128,320]{0,1:T(8,128)(2,1)S(1)}, u32[]{:S(2)}, u32[]{:S(2)}) %collective-permute-start.13) | collective-permute-done | bytes 81952 | tf_op jit(solution)/shard_map/gather_sequence/ppermute | solution.py:30
  115.5 1.9 collective-permute-start.14
  118.1 6.3 %collective-permute-done.14 = bf16[128,320]{0,1:T(8,128)(2,1)S(1)} collective-permute-done((bf16[128,320]{0,1:T(8,128)(2,1)S(1)}, bf16[128,320]{0,1:T(8,128)(2,1)S(1)}, u32[]{:S(2)}, u32[]{:S(2)}) %collective-permute-start.14) | collective-permute-done | bytes 81952 | tf_op jit(solution)/shard_map/gather_sequence/ppermute | solution.py:30
  129.6 3.5 %collective-permute-start.15 = (bf16[2048,320]{0,1:T(8,128)(2,1)}, bf16[2048,320]{0,1:T(8,128)(2,1)}, u32[]{:S(2)}, u32[]{:S(2)}) collective-permute-start(bf16[2048,320]{0,1:T(8,128)(2,1)} %constant_dynamic-update-slice_fusion), channel_id=1, source_target_pairs={{0,8},{8,16},{16,24},{24,0},{1,9},{9,17},{17,25},{25,1},{2,10},{10... | collective-permute-start | bytes 3932168 | tf_op jit(solution)/shard_map/gather_sequence/ppermute | solution.py:30
  133.2 3.7 %collective-permute-start.16 = (bf16[2048,320]{0,1:T(8,128)(2,1)}, bf16[2048,320]{0,1:T(8,128)(2,1)}, u32[]{:S(2)}, u32[]{:S(2)}) collective-permute-start(bf16[2048,320]{0,1:T(8,128)(2,1)} %constant_dynamic-update-slice_fusion), channel_id=1, source_target_pairs={{0,24},{8,0},{16,8},{24,16},{1,25},{9,1},{17,9},{25,17},{2,26},{10... | collective-permute-start | bytes 3932168 | tf_op jit(solution)/shard_map/gather_sequence/ppermute | solution.py:30
  136.9 2.2 %fusion.52 = (bf16[2048,160]{0,1:T(8,128)(2,1)}, bf16[2048,160]{0,1:T(8,128)(2,1)S(1)}) fusion(bf16[2048,320]{0,1:T(8,128)(2,1)} %constant_dynamic-update-slice_fusion), kind=kLoop, calls=%fused_computation.129 | loop fusion | bytes 2621440 | tf_op jit(solution)/shard_map/key_pass/slice | solution.py:163
  139.1 3.0 %fusion.51 = (bf16[8192,160]{0,1:T(8,128)(2,1)S(1)}, bf16[8192,160]{0,1:T(8,128)(2,1)S(1)}) fusion(bf16[8192,320]{0,1:T(8,128)(2,1)} %all-gather.2.cloned.1.call-done), kind=kLoop, calls=%fused_computation.128 | loop fusion | bytes 10485760 | tf_op jit(solution)/shard_map/gather_sequence/slice | solution.py:108
  143.9 2.5 %select_reduce_fusion = f32[2,128]{1,0:T(2,128)S(1)} fusion(f32[2,128,8192]{2,1,0:T(8,128)S(1)} %get-tuple-element.70, f32[2,128]{1,0:T(2,128)S(1)} %get-tuple-element.69, pred[128,8192]{1,0:T(8,128)(4,1)S(1)} %broadcast_compare_fusion), kind=kLoop, calls=%fused_computation.4 | loop fusion | flops 8388352 | bytes 9439232 | tf_op jit(solution)/shard_map/query_pass/reduce_sum | solution.py:128
  146.4 3.5 %fusion.57 = (f32[2,128]{1,0:T(2,128)S(1)}, bf16[2,128,8192]{2,1,0:T(8,128)(2,1)S(1)}) fusion(bf16[128,2,80]{0,2,1:T(8,128)(2,1)S(1)} %bitcast.192, bf16[8192,2,80]{0,2,1:T(8,128)(2,1)S(1)} %bitcast.178, f32[2,128,8192]{2,1,0:T(8,128)S(1)} %get-tuple-element.70, f32[2,128]{1,0:T(2,128)S(1)} %log_add_fusion, pred[128,8192]{1,0:T(8,128)(4,1)S(1)} %broadcast_compare_fusion), kind=kOutput, calls=%fused_computation.134 | convolution fusion | flops 346029824 | bytes 16295936 | tf_op jit(solution)/shard_map/query_pass/qhd,khd->hqk/dot_general | solution.py:131
  149.9 2.0 fusion.38
  155.3 8.6 %all-to-all-start = ((f32[64,2,2,128]{3,2,1,0:T(2,128)}), f32[64,2,2,128]{3,2,1,0:T(2,128)}, u32[]{:S(2)}, u32[]{:S(2)}) async-start(f32[64,2,2,128]{3,2,1,0:T(2,128)} %broadcast_in_dim.87), calls=%async_computation | async-start | bytes 262144 | tf_op jit(solution)/shard_map/gather_row_stats/all_to_all | solution.py:153
  164.0 2.0 slice.137
  166.0 3.4 %collective-permute-start.17 = (bf16[1024,320]{0,1:T(8,128)(2,1)}, bf16[1024,320]{0,1:T(8,128)(2,1)}, u32[]{:S(2)}, u32[]{:S(2)}) collective-permute-start(bf16[1024,320]{0,1:T(8,128)(2,1)} %slice.137), channel_id=1, source_target_pairs={{0,8},{8,16},{16,24},{24,0},{1,9},{9,17},{17,25},{25,1},{2,10},{10... | collective-permute-start | bytes 1966088 | tf_op jit(solution)/shard_map/gather_row_stats/ppermute | solution.py:30
  169.4 2.0 slice.138
  171.4 3.9 %collective-permute-start.18 = (bf16[1024,320]{0,1:T(8,128)(2,1)}, bf16[1024,320]{0,1:T(8,128)(2,1)}, u32[]{:S(2)}, u32[]{:S(2)}) collective-permute-start(bf16[1024,320]{0,1:T(8,128)(2,1)} %slice.138), channel_id=1, source_target_pairs={{0,24},{8,0},{16,8},{24,16},{1,25},{9,1},{17,9},{25,17},{2,26},{10... | collective-permute-start | bytes 1966088 | tf_op jit(solution)/shard_map/gather_row_stats/ppermute | solution.py:30
  175.3 3.0 %fusion.53 = (bf16[2048,160]{0,1:T(8,128)(2,1)}, bf16[2048,160]{0,1:T(8,128)(2,1)S(1)}, bf16[2048,160]{0,1:T(8,128)(2,1)S(1)}, bf16[2048,160]{0,1:T(8,128)(2,1)}) fusion(bf16[2048,320]{0,1:T(8,128)(2,1)} %collective-permute-done.16, bf16[2048,320]{0,1:T(8,128)(2,1)} %collective-permute-done.15), kind=kLoop, calls=%fused_computation.130 | loop fusion | bytes 5242880 | tf_op jit(solution)/shard_map/key_pass/slice | solution.py:163
  180.0 2.3 %gather_fusion.1 = f32[64,2,2,128]{3,2,1,0:T(2,128)} fusion(f32[64,2,2,128]{3,2,1,0:T(2,128)} %all-to-all-done, s32[1024]{0:T(1024)S(1)} %pad_clamp_fusion), kind=kCustom, calls=%fused_computation.1 | custom fusion | bytes 262400 | tf_op jit(solution)/shard_map/key_pass/gather | solution.py:156
  198.0 13.8 %all_to_all.10 = f32[4,129,320]{2,1,0:T(8,128)S(1)} all-to-all(f32[4,129,320]{2,1,0:T(8,128)S(1)} %copy.31), channel_id=1, replica_groups=mesh['z'=16,'y'=4,'tp'=4,'dp'=2] {'tp'}, dimensions={0} | all-to-all | bytes 1320960 | tf_op jit(solution)/shard_map/back_projection/all_to_all | solution.py:197
  (142 shorter events, 49.5 us)
Async XLA Ops:
  6.5 17.4 %copy-start = (bf16[160,1280]{1,0:T(8,128)(2,1)S(1)}, bf16[160,1280]{1,0:T(8,128)(2,1)}, u32[]{:S(2)}) copy-start(bf16[160,1280]{1,0:T(8,128)(2,1)} %param.16) | copy-start | bytes 1228804
  6.5 132.6 %all-gather.2.cloned.1.call-start = ((), (), s32[]{:S(2)}) async-start(), calls=%async_computation.2 | async-start | bytes 5570560 | tf_op jit(solution)/shard_map/gather_sequence/all_gather | solution.py:104
  7.5 16.3 %copy-start.15 = (f32[1280]{0:T(1024)S(1)}, f32[1280]{0:T(1024)}, u32[]{:S(2)}) copy-start(f32[1280]{0:T(1024)} %param.13) | copy-start | bytes 15364
  23.6 13.5 %copy-start.16 = (f32[80]{0:T(128)S(1)}, f32[80]{0:T(128)}, u32[]{:S(2)}) copy-start(f32[80]{0:T(128)} %param.18) | copy-start | bytes 964
  23.6 13.6 %copy-start.12 = (bf16[160,1280]{1,0:T(8,128)(2,1)S(1)}, bf16[160,1280]{1,0:T(8,128)(2,1)}, u32[]{:S(2)}) copy-start(bf16[160,1280]{1,0:T(8,128)(2,1)} %param.17) | copy-start | bytes 1228804
  23.8 13.6 %copy-start.7 = (bf16[160,1280]{1,0:T(8,128)(2,1)S(1)}, bf16[160,1280]{1,0:T(8,128)(2,1)}, u32[]{:S(2)}) copy-start(bf16[160,1280]{1,0:T(8,128)(2,1)} %param.14) | copy-start | bytes 1228804
  24.0 27.3 %copy-start.1 = (s32[64]{0:T(128)S(1)}, s32[64]{0:T(128)}, u32[]{:S(2)}) copy-start(s32[64]{0:T(128)} %param.19) | copy-start | bytes 772
  38.4 17.4 %collective-permute-start = (bf16[128,320]{0,1:T(8,128)(2,1)S(1)}, bf16[128,320]{0,1:T(8,128)(2,1)S(1)}, u32[]{:S(2)}, u32[]{:S(2)}) collective-permute-start(bf16[128,320]{0,1:T(8,128)(2,1)S(1)} %get-tuple-element.59), channel_id=1, source_target_pairs={{0,480},{32,0},{64,32},{96,64},{128,96},{160,128},{192,160},{224,1... | collective-permute-start | bytes 245768 | tf_op jit(solution)/shard_map/gather_sequence/ppermute | solution.py:30
  49.1 11.7 %collective-permute-start.7 = (bf16[128,320]{0,1:T(8,128)(2,1)S(1)}, bf16[128,320]{0,1:T(8,128)(2,1)S(1)}, u32[]{:S(2)}, u32[]{:S(2)}) collective-permute-start(bf16[128,320]{0,1:T(8,128)(2,1)S(1)} %get-tuple-element.59), channel_id=1, source_target_pairs={{0,32},{32,64},{64,96},{96,128},{128,160},{160,192},{192,224},{224... | collective-permute-start | bytes 245768 | tf_op jit(solution)/shard_map/gather_sequence/ppermute | solution.py:30
  55.8 8.7 %collective-permute-start.1 = (bf16[128,320]{0,1:T(8,128)(2,1)S(1)}, bf16[128,320]{0,1:T(8,128)(2,1)S(1)}, u32[]{:S(2)}, u32[]{:S(2)}) collective-permute-start(bf16[128,320]{0,1:T(8,128)(2,1)S(1)} %collective-permute-done), channel_id=1, source_target_pairs={{0,480},{32,0},{64,32},{96,64},{128,96},{160,128},{192,160},{224,1... | collective-permute-start | bytes 245768 | tf_op jit(solution)/shard_map/gather_sequence/ppermute | solution.py:30
  60.9 9.6 %collective-permute-start.8 = (bf16[128,320]{0,1:T(8,128)(2,1)S(1)}, bf16[128,320]{0,1:T(8,128)(2,1)S(1)}, u32[]{:S(2)}, u32[]{:S(2)}) collective-permute-start(bf16[128,320]{0,1:T(8,128)(2,1)S(1)} %collective-permute-done.7), channel_id=1, source_target_pairs={{0,32},{32,64},{64,96},{96,128},{128,160},{160,192},{192,224},{224... | collective-permute-start | bytes 245768 | tf_op jit(solution)/shard_map/gather_sequence/ppermute | solution.py:30
  64.5 8.9 %collective-permute-start.2 = (bf16[128,320]{0,1:T(8,128)(2,1)S(1)}, bf16[128,320]{0,1:T(8,128)(2,1)S(1)}, u32[]{:S(2)}, u32[]{:S(2)}) collective-permute-start(bf16[128,320]{0,1:T(8,128)(2,1)S(1)} %collective-permute-done.1), channel_id=1, source_target_pairs={{0,480},{32,0},{64,32},{96,64},{128,96},{160,128},{192,160},{224,1... | collective-permute-start | bytes 245768 | tf_op jit(solution)/shard_map/gather_sequence/ppermute | solution.py:30
  70.5 9.2 %collective-permute-start.9 = (bf16[128,320]{0,1:T(8,128)(2,1)S(1)}, bf16[128,320]{0,1:T(8,128)(2,1)S(1)}, u32[]{:S(2)}, u32[]{:S(2)}) collective-permute-start(bf16[128,320]{0,1:T(8,128)(2,1)S(1)} %collective-permute-done.8), channel_id=1, source_target_pairs={{0,32},{32,64},{64,96},{96,128},{128,160},{160,192},{192,224},{224... | collective-permute-start | bytes 245768 | tf_op jit(solution)/shard_map/gather_sequence/ppermute | solution.py:30
  73.3 9.3 %collective-permute-start.3 = (bf16[128,320]{0,1:T(8,128)(2,1)S(1)}, bf16[128,320]{0,1:T(8,128)(2,1)S(1)}, u32[]{:S(2)}, u32[]{:S(2)}) collective-permute-start(bf16[128,320]{0,1:T(8,128)(2,1)S(1)} %collective-permute-done.2), channel_id=1, source_target_pairs={{0,480},{32,0},{64,32},{96,64},{128,96},{160,128},{192,160},{224,1... | collective-permute-start | bytes 245768 | tf_op jit(solution)/shard_map/gather_sequence/ppermute | solution.py:30
  79.7 9.1 %collective-permute-start.10 = (bf16[128,320]{0,1:T(8,128)(2,1)S(1)}, bf16[128,320]{0,1:T(8,128)(2,1)S(1)}, u32[]{:S(2)}, u32[]{:S(2)}) collective-permute-start(bf16[128,320]{0,1:T(8,128)(2,1)S(1)} %collective-permute-done.9), channel_id=1, source_target_pairs={{0,32},{32,64},{64,96},{96,128},{128,160},{160,192},{192,224},{224... | collective-permute-start | bytes 245768 | tf_op jit(solution)/shard_map/gather_sequence/ppermute | solution.py:30
  82.7 8.9 %collective-permute-start.4 = (bf16[128,320]{0,1:T(8,128)(2,1)S(1)}, bf16[128,320]{0,1:T(8,128)(2,1)S(1)}, u32[]{:S(2)}, u32[]{:S(2)}) collective-permute-start(bf16[128,320]{0,1:T(8,128)(2,1)S(1)} %collective-permute-done.3), channel_id=1, source_target_pairs={{0,480},{32,0},{64,32},{96,64},{128,96},{160,128},{192,160},{224,1... | collective-permute-start | bytes 245768 | tf_op jit(solution)/shard_map/gather_sequence/ppermute | solution.py:30
  88.9 9.0 %collective-permute-start.11 = (bf16[128,320]{0,1:T(8,128)(2,1)S(1)}, bf16[128,320]{0,1:T(8,128)(2,1)S(1)}, u32[]{:S(2)}, u32[]{:S(2)}) collective-permute-start(bf16[128,320]{0,1:T(8,128)(2,1)S(1)} %collective-permute-done.10), channel_id=1, source_target_pairs={{0,32},{32,64},{64,96},{96,128},{128,160},{160,192},{192,224},{224... | collective-permute-start | bytes 245768 | tf_op jit(solution)/shard_map/gather_sequence/ppermute | solution.py:30
  91.5 8.9 %collective-permute-start.5 = (bf16[128,320]{0,1:T(8,128)(2,1)S(1)}, bf16[128,320]{0,1:T(8,128)(2,1)S(1)}, u32[]{:S(2)}, u32[]{:S(2)}) collective-permute-start(bf16[128,320]{0,1:T(8,128)(2,1)S(1)} %collective-permute-done.4), channel_id=1, source_target_pairs={{0,480},{32,0},{64,32},{96,64},{128,96},{160,128},{192,160},{224,1... | collective-permute-start | bytes 245768 | tf_op jit(solution)/shard_map/gather_sequence/ppermute | solution.py:30
  97.8 8.9 %collective-permute-start.12 = (bf16[128,320]{0,1:T(8,128)(2,1)S(1)}, bf16[128,320]{0,1:T(8,128)(2,1)S(1)}, u32[]{:S(2)}, u32[]{:S(2)}) collective-permute-start(bf16[128,320]{0,1:T(8,128)(2,1)S(1)} %collective-permute-done.11), channel_id=1, source_target_pairs={{0,32},{32,64},{64,96},{96,128},{128,160},{160,192},{192,224},{224... | collective-permute-start | bytes 245768 | tf_op jit(solution)/shard_map/gather_sequence/ppermute | solution.py:30
  100.4 17.0 %collective-permute-start.6 = (bf16[128,320]{0,1:T(8,128)(2,1)S(1)}, bf16[128,320]{0,1:T(8,128)(2,1)S(1)}, u32[]{:S(2)}, u32[]{:S(2)}) collective-permute-start(bf16[128,320]{0,1:T(8,128)(2,1)S(1)} %collective-permute-done.5), channel_id=1, source_target_pairs={{0,480},{32,0},{64,32},{96,64},{128,96},{160,128},{192,160},{224,1... | collective-permute-start | bytes 245768 | tf_op jit(solution)/shard_map/gather_sequence/ppermute | solution.py:30
  106.7 8.8 %collective-permute-start.13 = (bf16[128,320]{0,1:T(8,128)(2,1)S(1)}, bf16[128,320]{0,1:T(8,128)(2,1)S(1)}, u32[]{:S(2)}, u32[]{:S(2)}) collective-permute-start(bf16[128,320]{0,1:T(8,128)(2,1)S(1)} %collective-permute-done.12), channel_id=1, source_target_pairs={{0,32},{32,64},{64,96},{96,128},{128,160},{160,192},{192,224},{224... | collective-permute-start | bytes 245768 | tf_op jit(solution)/shard_map/gather_sequence/ppermute | solution.py:30
  115.5 8.9 %collective-permute-start.14 = (bf16[128,320]{0,1:T(8,128)(2,1)S(1)}, bf16[128,320]{0,1:T(8,128)(2,1)S(1)}, u32[]{:S(2)}, u32[]{:S(2)}) collective-permute-start(bf16[128,320]{0,1:T(8,128)(2,1)S(1)} %collective-permute-done.13), channel_id=1, source_target_pairs={{0,32},{32,64},{64,96},{96,128},{128,160},{160,192},{192,224},{224... | collective-permute-start | bytes 245768 | tf_op jit(solution)/shard_map/gather_sequence/ppermute | solution.py:30
  129.6 25.0 %collective-permute-start.15 = (bf16[2048,320]{0,1:T(8,128)(2,1)}, bf16[2048,320]{0,1:T(8,128)(2,1)}, u32[]{:S(2)}, u32[]{:S(2)}) collective-permute-start(bf16[2048,320]{0,1:T(8,128)(2,1)} %constant_dynamic-update-slice_fusion), channel_id=1, source_target_pairs={{0,8},{8,16},{16,24},{24,0},{1,9},{9,17},{17,25},{25,1},{2,10},{10... | collective-permute-start | bytes 3932168 | tf_op jit(solution)/shard_map/gather_sequence/ppermute | solution.py:30
  133.2 21.5 %collective-permute-start.16 = (bf16[2048,320]{0,1:T(8,128)(2,1)}, bf16[2048,320]{0,1:T(8,128)(2,1)}, u32[]{:S(2)}, u32[]{:S(2)}) collective-permute-start(bf16[2048,320]{0,1:T(8,128)(2,1)} %constant_dynamic-update-slice_fusion), channel_id=1, source_target_pairs={{0,24},{8,0},{16,8},{24,16},{1,25},{9,1},{17,9},{25,17},{2,26},{10... | collective-permute-start | bytes 3932168 | tf_op jit(solution)/shard_map/gather_sequence/ppermute | solution.py:30
  151.9 1.7 copy-start.8
  155.3 24.7 %all-to-all-start = ((f32[64,2,2,128]{3,2,1,0:T(2,128)}), f32[64,2,2,128]{3,2,1,0:T(2,128)}, u32[]{:S(2)}, u32[]{:S(2)}) async-start(f32[64,2,2,128]{3,2,1,0:T(2,128)} %broadcast_in_dim.87), calls=%async_computation | async-start | bytes 262144 | tf_op jit(solution)/shard_map/gather_row_stats/all_to_all | solution.py:153
  166.0 24.6 %collective-permute-start.17 = (bf16[1024,320]{0,1:T(8,128)(2,1)}, bf16[1024,320]{0,1:T(8,128)(2,1)}, u32[]{:S(2)}, u32[]{:S(2)}) collective-permute-start(bf16[1024,320]{0,1:T(8,128)(2,1)} %slice.137), channel_id=1, source_target_pairs={{0,8},{8,16},{16,24},{24,0},{1,9},{9,17},{17,25},{25,1},{2,10},{10... | collective-permute-start | bytes 1966088 | tf_op jit(solution)/shard_map/gather_row_stats/ppermute | solution.py:30
  171.4 20.4 %collective-permute-start.18 = (bf16[1024,320]{0,1:T(8,128)(2,1)}, bf16[1024,320]{0,1:T(8,128)(2,1)}, u32[]{:S(2)}, u32[]{:S(2)}) collective-permute-start(bf16[1024,320]{0,1:T(8,128)(2,1)} %slice.138), channel_id=1, source_target_pairs={{0,24},{8,0},{16,8},{24,16},{1,25},{9,1},{17,9},{25,17},{2,26},{10... | collective-permute-start | bytes 1966088 | tf_op jit(solution)/shard_map/gather_row_stats/ppermute | solution.py:30
  183.1 1.8 copy-start.3
  191.8 1.3 copy-start.9
  198.0 14.0 %copy-start.13 = (bf16[128,320]{0,1:T(8,128)(2,1)S(1)}, bf16[128,320]{0,1:T(8,128)(2,1)}, u32[]{:S(2)}) copy-start(bf16[128,320]{0,1:T(8,128)(2,1)} %param.11) | copy-start | bytes 245764
  198.0 14.0 %copy-start.14 = (bf16[128,320]{0,1:T(8,128)(2,1)S(1)}, bf16[128,320]{0,1:T(8,128)(2,1)}, u32[]{:S(2)}) copy-start(bf16[128,320]{0,1:T(8,128)(2,1)} %param.12) | copy-start | bytes 245764
  (6 other events, 6.3 us)
Sparse Core Ops, SparseCore 0:
  37.1 91.6 all-gather.1
where the time goes:
time: 221 us; the launch traced here: 220 us
  starting transfers between devices  82.2 us (37%)
  blocking collectives  41.9 us (19%)
  local copies, waits for them, and re-layouts  31.9 us (14%)
  matrix products  21.5 us (10%)
  waiting for transfers between devices  19.3 us (9%)
  between operations  14.8 us (7%)
  other arithmetic  7.99 us (4%)
    ppermute x19, starting transfers between devices, shift(): lax.ppermute(data, axis, [(i, (i + step) % size) for i in range(size)])  73.6 us
    ppermute x19, waiting for transfers between devices, shift(): lax.ppermute(data, axis, [(i, (i + step) % size) for i in range(size)])  17.5 us
    all_gather x1, blocking collectives, per_device(): gathered = lax.all_gather(both, 'tp', axis=1, tiled=True)  15.7 us
    all_to_all x1, blocking collectives, per_device(): received = lax.all_to_all(payload, 'tp', 0, 0, tiled=False)  13.8 us
    all_gather x1, blocking collectives, per_device(): kv_all = lax.all_gather(kv, 'y', axis=0, tiled=True)  12.3 us
    unnamed x50, local copies, waits for them, and re-layouts  11.4 us
    all_to_all x1, starting transfers between devices, per_device(): stats_all = lax.all_to_all(sent, ('z', 'y'), 0, 0, tiled=False)  8.64 us
    slice x3, local copies, waits for them, and re-layouts, per_device(): grad_part = piece[:, cols:].reshape(piece_rows, heads_here, head_width)  5.4 us
  transfers between devices with their start and end apart: 21, of which 12 were waited for; matrix products, arithmetic and copies ran while one was open for 23% of the time, Pallas kernels for 0%

commit v1 on v0

--- a/solution.py
+++ b/solution.py
@@ -71,7 +71,29 @@
     contract = (((1,), (1,)), ((), ()))
     with jax.named_scope("gather_features"):
         both = jnp.concatenate([inputs, out_grads], axis=1)
-        gathered = lax.all_gather(both, "tp", axis=1, tiled=True)
+        arr_now = lax.axis_size("tp")
+        built = lax.axis_index("tp")
+        formed, outcome_arr, current_value = (arr_now, built, both.shape[1])
+        row_list = tuple(((u, (u + 1) % formed) for u in range(formed)))
+        trail = tuple(((u, (u - 1) % formed) for u in range(formed)))
+        gathered = jnp.zeros(
+            (*both.shape[:1], formed * current_value, *both.shape[1 + 1 :]), both.dtype
+        )
+        gathered = lax.dynamic_update_slice_in_dim(
+            gathered, both, outcome_arr * current_value, axis=1
+        )
+        taken_in = reached = both
+        last = formed // 2
+        for c in range(1, last + 1):
+            taken_in = lax.ppermute(taken_in, axis_name="tp", perm=row_list)
+            gathered = lax.dynamic_update_slice_in_dim(
+                gathered, taken_in, (outcome_arr - c) % formed * current_value, axis=1
+            )
+            if c < formed - last:
+                reached = lax.ppermute(reached, axis_name="tp", perm=trail)
+                gathered = lax.dynamic_update_slice_in_dim(
+                    gathered, reached, (outcome_arr + c) % formed * current_value, axis=1
+                )
         gathered = gathered.reshape(row_count, tp_size, 2, width_here)
         full_inputs = gathered[:, :, 0, :].reshape(row_count, tp_size * width_here)
         full_grads = gathered[:, :, 1, :].reshape(row_count, tp_size * width_here)

time: 221 us -> 229 us (1.036)
  blocking collectives: 41.9 us -> 25.7 us
  waiting for transfers between devices: 19.3 us -> 29.4 us
  starting transfers between devices: 82.2 us -> 92.1 us
    all_gather x1 -> x0, blocking collectives: 15.7 us -> none  [per_device(): gathered = lax.all_gather(both, 'tp', axis=1, tiled=True)]
    ppermute x0 -> x3, starting transfers between devices: none -> 11.6 us  [the longest x1 6.34 us: per_device(): reached = lax.ppermute(reached, axis_name='tp', perm=trail)]
    ppermute x0 -> x3, waiting for transfers between devices: none -> 8.81 us  [the longest x2 8.8 us: per_device(): taken_in = lax.ppermute(taken_in, axis_name='tp', perm=row_list)]
    ppermute x19, starting transfers between devices: 73.6 us -> 70.9 us  [shift(): lax.ppermute(data, axis, [(i, (i + step) % size) for i in range(size)])]
    unnamed x50 -> x47, local copies, waits for them, and re-layouts: 11.4 us -> 12.3 us
  transfers between devices with their start and end apart: 21 -> 24, of which waited for: 12 -> 16; matrix products, arithmetic and copies ran while one was open for 23% -> 23% of each run, Pallas kernels for 0% -> 0%
where the time goes in v1:
time: 229 us; the launch traced here: 227 us
  starting transfers between devices  92.1 us (40%)
  local copies, waits for them, and re-layouts  33.9 us (15%)
  waiting for transfers between devices  29.4 us (13%)
  blocking collectives  25.7 us (11%)
  matrix products  23.6 us (10%)
  between operations  14.9 us (7%)
  other arithmetic  7.74 us (3%)
    ppermute x19, starting transfers between devices, shift(): lax.ppermute(data, axis, [(i, (i + step) % size) for i in range(size)])  70.9 us
    ppermute x19, waiting for transfers between devices, shift(): lax.ppermute(data, axis, [(i, (i + step) % size) for i in range(size)])  18.8 us
    all_to_all x1, blocking collectives, per_device(): received = lax.all_to_all(payload, 'tp', 0, 0, tiled=False)  13.7 us
    unnamed x47, local copies, waits for them, and re-layouts  12.3 us
    all_gather x1, blocking collectives, per_device(): kv_all = lax.all_gather(kv, 'y', axis=0, tiled=True)  12 us
    all_to_all x1, starting transfers between devices, per_device(): stats_all = lax.all_to_all(sent, ('z', 'y'), 0, 0, tiled=False)  9.52 us
    ppermute x2, waiting for transfers between devices, per_device(): taken_in = lax.ppermute(taken_in, axis_name='tp', perm=row_list)  8.8 us
    ppermute x1, starting transfers between devices, per_device(): reached = lax.ppermute(reached, axis_name='tp', perm=trail)  6.34 us
  transfers between devices with their start and end apart: 24, of which 16 were waited for; matrix products, arithmetic and copies ran while one was open for 23% of the time, Pallas kernels for 0%

profile of v1, /device:TPU:2, one launch (start us, length us, event | category | flops | bytes accessed | tf_op | source)
XLA Modules:
  0.0 227.4 jit_solution(14965207491659823071)
XLA Ops:
  8.4 3.4 %collective-permute-start = (bf16[128,640]{0,1:T(8,128)(2,1)S(1)}, bf16[128,640]{0,1:T(8,128)(2,1)S(1)}, u32[]{:S(2)}, u32[]{:S(2)}) collective-permute-start(bf16[128,640]{0,1:T(8,128)(2,1)S(1)} %constant_dynamic-update-slice_fusion), channel_id=1, source_target_pairs={{0,2},{2,4},{4,6},{6,0},{1,3},{3,5},{5,7},{7,1},{8,10},{10,12},{12... | collective-permute-start | bytes 491528 | tf_op jit(solution)/shard_map/gather_features/ppermute | solution.py:88
  11.8 6.3 %collective-permute-start.1 = (bf16[128,640]{0,1:T(8,128)(2,1)S(1)}, bf16[128,640]{0,1:T(8,128)(2,1)S(1)}, u32[]{:S(2)}, u32[]{:S(2)}) collective-permute-start(bf16[128,640]{0,1:T(8,128)(2,1)S(1)} %constant_dynamic-update-slice_fusion), channel_id=1, source_target_pairs={{0,6},{2,0},{4,2},{6,4},{1,7},{3,1},{5,3},{7,5},{8,14},{10,8},{12,... | collective-permute-start | bytes 491528 | tf_op jit(solution)/shard_map/gather_features/ppermute | solution.py:93
  22.2 6.9 %collective-permute-done.2 = bf16[128,640]{0,1:T(8,128)(2,1)S(1)} collective-permute-done((bf16[128,640]{0,1:T(8,128)(2,1)S(1)}, bf16[128,640]{0,1:T(8,128)(2,1)S(1)}, u32[]{:S(2)}, u32[]{:S(2)}) %collective-permute-start.2) | collective-permute-done | bytes 163872 | tf_op jit(solution)/shard_map/gather_features/ppermute | solution.py:88
  31.3 12.0 %all_gather.6 = bf16[512,320]{0,1:T(8,128)(2,1)} all-gather(bf16[128,320]{0,1:T(8,128)(2,1)S(1)} %pad_maximum_fusion.1), channel_id=1, replica_groups=mesh['z'=16,'y'=4,'tp'=4,'dp'=2] {'y'}, dimensions={0}, use_global_device_ids=true | all-gather | bytes 409600 | tf_op jit(solution)/shard_map/gather_sequence/all_gather | solution.py:125
  49.7 7.6 %collective-permute-start.3 = (bf16[128,320]{0,1:T(8,128)(2,1)S(1)}, bf16[128,320]{0,1:T(8,128)(2,1)S(1)}, u32[]{:S(2)}, u32[]{:S(2)}) collective-permute-start(bf16[128,320]{0,1:T(8,128)(2,1)S(1)} %get-tuple-element.59), channel_id=1, source_target_pairs={{0,480},{32,0},{64,32},{96,64},{128,96},{160,128},{192,160},{224,1... | collective-permute-start | bytes 245768 | tf_op jit(solution)/shard_map/gather_sequence/ppermute | solution.py:30
  57.4 1.9 collective-permute-start.10
  61.3 5.6 %collective-permute-start.4 = (bf16[128,320]{0,1:T(8,128)(2,1)S(1)}, bf16[128,320]{0,1:T(8,128)(2,1)S(1)}, u32[]{:S(2)}, u32[]{:S(2)}) collective-permute-start(bf16[128,320]{0,1:T(8,128)(2,1)S(1)} %collective-permute-done.3), channel_id=1, source_target_pairs={{0,480},{32,0},{64,32},{96,64},{128,96},{160,128},{192,160},{224,1... | collective-permute-start | bytes 245768 | tf_op jit(solution)/shard_map/gather_sequence/ppermute | solution.py:30
  66.9 1.9 collective-permute-start.11
  70.9 5.6 %collective-permute-start.5 = (bf16[128,320]{0,1:T(8,128)(2,1)S(1)}, bf16[128,320]{0,1:T(8,128)(2,1)S(1)}, u32[]{:S(2)}, u32[]{:S(2)}) collective-permute-start(bf16[128,320]{0,1:T(8,128)(2,1)S(1)} %collective-permute-done.4), channel_id=1, source_target_pairs={{0,480},{32,0},{64,32},{96,64},{128,96},{160,128},{192,160},{224,1... | collective-permute-start | bytes 245768 | tf_op jit(solution)/shard_map/gather_sequence/ppermute | solution.py:30
  76.8 1.9 collective-permute-start.12
  80.6 5.6 %collective-permute-start.6 = (bf16[128,320]{0,1:T(8,128)(2,1)S(1)}, bf16[128,320]{0,1:T(8,128)(2,1)S(1)}, u32[]{:S(2)}, u32[]{:S(2)}) collective-permute-start(bf16[128,320]{0,1:T(8,128)(2,1)S(1)} %collective-permute-done.5), channel_id=1, source_target_pairs={{0,480},{32,0},{64,32},{96,64},{128,96},{160,128},{192,160},{224,1... | collective-permute-start | bytes 245768 | tf_op jit(solution)/shard_map/gather_sequence/ppermute | solution.py:30
  86.2 1.9 collective-permute-start.13
  89.7 5.6 %collective-permute-start.7 = (bf16[128,320]{0,1:T(8,128)(2,1)S(1)}, bf16[128,320]{0,1:T(8,128)(2,1)S(1)}, u32[]{:S(2)}, u32[]{:S(2)}) collective-permute-start(bf16[128,320]{0,1:T(8,128)(2,1)S(1)} %collective-permute-done.6), channel_id=1, source_target_pairs={{0,480},{32,0},{64,32},{96,64},{128,96},{160,128},{192,160},{224,1... | collective-permute-start | bytes 245768 | tf_op jit(solution)/shard_map/gather_sequence/ppermute | solution.py:30
  98.6 5.6 %collective-permute-start.8 = (bf16[128,320]{0,1:T(8,128)(2,1)S(1)}, bf16[128,320]{0,1:T(8,128)(2,1)S(1)}, u32[]{:S(2)}, u32[]{:S(2)}) collective-permute-start(bf16[128,320]{0,1:T(8,128)(2,1)S(1)} %collective-permute-done.7), channel_id=1, source_target_pairs={{0,480},{32,0},{64,32},{96,64},{128,96},{160,128},{192,160},{224,1... | collective-permute-start | bytes 245768 | tf_op jit(solution)/shard_map/gather_sequence/ppermute | solution.py:30
  107.6 5.6 %collective-permute-start.9 = (bf16[128,320]{0,1:T(8,128)(2,1)S(1)}, bf16[128,320]{0,1:T(8,128)(2,1)S(1)}, u32[]{:S(2)}, u32[]{:S(2)}) collective-permute-start(bf16[128,320]{0,1:T(8,128)(2,1)S(1)} %collective-permute-done.8), channel_id=1, source_target_pairs={{0,480},{32,0},{64,32},{96,64},{128,96},{160,128},{192,160},{224,1... | collective-permute-start | bytes 245768 | tf_op jit(solution)/shard_map/gather_sequence/ppermute | solution.py:30
  116.2 6.3 %collective-permute-done.16 = bf16[128,320]{0,1:T(8,128)(2,1)S(1)} collective-permute-done((bf16[128,320]{0,1:T(8,128)(2,1)S(1)}, bf16[128,320]{0,1:T(8,128)(2,1)S(1)}, u32[]{:S(2)}, u32[]{:S(2)}) %collective-permute-start.16) | collective-permute-done | bytes 81952 | tf_op jit(solution)/shard_map/gather_sequence/ppermute | solution.py:30
  125.1 5.4 %collective-permute-done.17 = bf16[128,320]{0,1:T(8,128)(2,1)S(1)} collective-permute-done((bf16[128,320]{0,1:T(8,128)(2,1)S(1)}, bf16[128,320]{0,1:T(8,128)(2,1)S(1)}, u32[]{:S(2)}, u32[]{:S(2)}) %collective-permute-start.17) | collective-permute-done | bytes 81952 | tf_op jit(solution)/shard_map/gather_sequence/ppermute | solution.py:30
  135.7 2.5 %collective-permute-start.18 = (bf16[2048,320]{0,1:T(8,128)(2,1)}, bf16[2048,320]{0,1:T(8,128)(2,1)}, u32[]{:S(2)}, u32[]{:S(2)}) collective-permute-start(bf16[2048,320]{0,1:T(8,128)(2,1)} %constant_dynamic-update-slice_fusion.2), channel_id=1, source_target_pairs={{0,8},{8,16},{16,24},{24,0},{1,9},{9,17},{17,25},{25,1},{2,10},{10... | collective-permute-start | bytes 3932168 | tf_op jit(solution)/shard_map/gather_sequence/ppermute | solution.py:30
  138.2 4.8 %collective-permute-start.19 = (bf16[2048,320]{0,1:T(8,128)(2,1)}, bf16[2048,320]{0,1:T(8,128)(2,1)}, u32[]{:S(2)}, u32[]{:S(2)}) collective-permute-start(bf16[2048,320]{0,1:T(8,128)(2,1)} %constant_dynamic-update-slice_fusion.2), channel_id=1, source_target_pairs={{0,24},{8,0},{16,8},{24,16},{1,25},{9,1},{17,9},{25,17},{2,26},{10... | collective-permute-start | bytes 3932168 | tf_op jit(solution)/shard_map/gather_sequence/ppermute | solution.py:30
  142.9 2.2 fusion.52
  145.2 3.0 %fusion.51 = (bf16[8192,160]{0,1:T(8,128)(2,1)S(1)}, bf16[8192,160]{0,1:T(8,128)(2,1)S(1)}) fusion(bf16[8192,320]{0,1:T(8,128)(2,1)} %all-gather.2.cloned.1.call-done), kind=kLoop, calls=%fused_computation.133 | loop fusion | bytes 10485760 | tf_op jit(solution)/shard_map/gather_sequence/slice | solution.py:130
  150.0 2.5 %select_reduce_fusion = f32[2,128]{1,0:T(2,128)S(1)} fusion(f32[2,128,8192]{2,1,0:T(8,128)S(1)} %get-tuple-element.70, f32[2,128]{1,0:T(2,128)S(1)} %get-tuple-element.69, pred[128,8192]{1,0:T(8,128)(4,1)S(1)} %broadcast_compare_fusion), kind=kLoop, calls=%fused_computation.4 | loop fusion | flops 8388352 | bytes 9439232 | tf_op jit(solution)/shard_map/query_pass/reduce_sum | solution.py:150
  152.5 3.5 %fusion.57 = (f32[2,128]{1,0:T(2,128)S(1)}, bf16[2,128,8192]{2,1,0:T(8,128)(2,1)S(1)}) fusion(bf16[128,2,80]{0,2,1:T(8,128)(2,1)S(1)} %bitcast.192, bf16[8192,2,80]{0,2,1:T(8,128)(2,1)S(1)} %bitcast.178, f32[2,128,8192]{2,1,0:T(8,128)S(1)} %get-tuple-element.70, f32[2,128]{1,0:T(2,128)S(1)} %log_add_fusion, pred[128,8192]{1,0:T(8,128)(4,1)S(1)} %broadcast_compare_fusion), kind=kOutput, calls=%fused_computation.139 | convolution fusion | flops 346029824 | bytes 16295936 | tf_op jit(solution)/shard_map/query_pass/qhd,khd->hqk/dot_general | solution.py:153
  156.0 2.0 fusion.38
  162.3 9.5 %all-to-all-start = ((f32[64,2,2,128]{3,2,1,0:T(2,128)}), f32[64,2,2,128]{3,2,1,0:T(2,128)}, u32[]{:S(2)}, u32[]{:S(2)}) async-start(f32[64,2,2,128]{3,2,1,0:T(2,128)} %broadcast_in_dim.91), calls=%async_computation | async-start | bytes 262144 | tf_op jit(solution)/shard_map/gather_row_stats/all_to_all | solution.py:175
  171.8 2.0 slice.137
  173.8 3.4 %collective-permute-start.20 = (bf16[1024,320]{0,1:T(8,128)(2,1)}, bf16[1024,320]{0,1:T(8,128)(2,1)}, u32[]{:S(2)}, u32[]{:S(2)}) collective-permute-start(bf16[1024,320]{0,1:T(8,128)(2,1)} %slice.137), channel_id=1, source_target_pairs={{0,8},{8,16},{16,24},{24,0},{1,9},{9,17},{17,25},{25,1},{2,10},{10... | collective-permute-start | bytes 1966088 | tf_op jit(solution)/shard_map/gather_row_stats/ppermute | solution.py:30
  177.2 2.0 slice.138
  179.2 3.9 %collective-permute-start.21 = (bf16[1024,320]{0,1:T(8,128)(2,1)}, bf16[1024,320]{0,1:T(8,128)(2,1)}, u32[]{:S(2)}, u32[]{:S(2)}) collective-permute-start(bf16[1024,320]{0,1:T(8,128)(2,1)} %slice.138), channel_id=1, source_target_pairs={{0,24},{8,0},{16,8},{24,16},{1,25},{9,1},{17,9},{25,17},{2,26},{10... | collective-permute-start | bytes 1966088 | tf_op jit(solution)/shard_map/gather_row_stats/ppermute | solution.py:30
  183.1 3.0 %fusion.53 = (bf16[2048,160]{0,1:T(8,128)(2,1)}, bf16[2048,160]{0,1:T(8,128)(2,1)S(1)}, bf16[2048,160]{0,1:T(8,128)(2,1)S(1)}, bf16[2048,160]{0,1:T(8,128)(2,1)}) fusion(bf16[2048,320]{0,1:T(8,128)(2,1)} %collective-permute-done.19, bf16[2048,320]{0,1:T(8,128)(2,1)} %collective-permute-done.18), kind=kLoop, calls=%fused_computation.135 | loop fusion | bytes 5242880 | tf_op jit(solution)/shard_map/key_pass/slice | solution.py:185
  187.9 2.3 gather_fusion.1
  205.9 13.7 %all_to_all.10 = f32[4,129,320]{2,1,0:T(8,128)S(1)} all-to-all(f32[4,129,320]{2,1,0:T(8,128)S(1)} %copy.27), channel_id=1, replica_groups=mesh['z'=16,'y'=4,'tp'=4,'dp'=2] {'tp'}, dimensions={0} | all-to-all | bytes 1320960 | tf_op jit(solution)/shard_map/back_projection/all_to_all | solution.py:219
  (149 shorter events, 63.2 us)
Async XLA Ops:
  6.5 24.0 %copy-start = (bf16[160,1280]{1,0:T(8,128)(2,1)S(1)}, bf16[160,1280]{1,0:T(8,128)(2,1)}, u32[]{:S(2)}) copy-start(bf16[160,1280]{1,0:T(8,128)(2,1)} %param.16) | copy-start | bytes 1228804
  6.5 138.6 %all-gather.2.cloned.1.call-start = ((), (), s32[]{:S(2)}) async-start(), calls=%async_computation.2 | async-start | bytes 5570560 | tf_op jit(solution)/shard_map/gather_sequence/all_gather | solution.py:126
  8.4 11.8 %collective-permute-start = (bf16[128,640]{0,1:T(8,128)(2,1)S(1)}, bf16[128,640]{0,1:T(8,128)(2,1)S(1)}, u32[]{:S(2)}, u32[]{:S(2)}) collective-permute-start(bf16[128,640]{0,1:T(8,128)(2,1)S(1)} %constant_dynamic-update-slice_fusion), channel_id=1, source_target_pairs={{0,2},{2,4},{4,6},{6,0},{1,3},{3,5},{5,7},{7,1},{8,10},{10,12},{12... | collective-permute-start | bytes 491528 | tf_op jit(solution)/shard_map/gather_features/ppermute | solution.py:88
  11.8 10.4 %collective-permute-start.1 = (bf16[128,640]{0,1:T(8,128)(2,1)S(1)}, bf16[128,640]{0,1:T(8,128)(2,1)S(1)}, u32[]{:S(2)}, u32[]{:S(2)}) collective-permute-start(bf16[128,640]{0,1:T(8,128)(2,1)S(1)} %constant_dynamic-update-slice_fusion), channel_id=1, source_target_pairs={{0,6},{2,0},{4,2},{6,4},{1,7},{3,1},{5,3},{7,5},{8,14},{10,8},{12,... | collective-permute-start | bytes 491528 | tf_op jit(solution)/shard_map/gather_features/ppermute | solution.py:93
  18.3 12.1 %copy-start.13 = (f32[1280]{0:T(1024)S(1)}, f32[1280]{0:T(1024)}, u32[]{:S(2)}) copy-start(f32[1280]{0:T(1024)} %param.13) | copy-start | bytes 15364
  20.2 8.9 %collective-permute-start.2 = (bf16[128,640]{0,1:T(8,128)(2,1)S(1)}, bf16[128,640]{0,1:T(8,128)(2,1)S(1)}, u32[]{:S(2)}, u32[]{:S(2)}) collective-permute-start(bf16[128,640]{0,1:T(8,128)(2,1)S(1)} %collective-permute-done), channel_id=1, source_target_pairs={{0,2},{2,4},{4,6},{6,0},{1,3},{3,5},{5,7},{7,1},{8,10},{10,12},{12... | collective-permute-start | bytes 491528 | tf_op jit(solution)/shard_map/gather_features/ppermute | solution.py:88
  30.2 13.1 %copy-start.14 = (f32[80]{0:T(128)S(1)}, f32[80]{0:T(128)}, u32[]{:S(2)}) copy-start(f32[80]{0:T(128)} %param.18) | copy-start | bytes 964
  30.2 13.4 %copy-start.1 = (s32[64]{0:T(128)S(1)}, s32[64]{0:T(128)}, u32[]{:S(2)}) copy-start(s32[64]{0:T(128)} %param.19) | copy-start | bytes 772
  49.7 11.5 %collective-permute-start.3 = (bf16[128,320]{0,1:T(8,128)(2,1)S(1)}, bf16[128,320]{0,1:T(8,128)(2,1)S(1)}, u32[]{:S(2)}, u32[]{:S(2)}) collective-permute-start(bf16[128,320]{0,1:T(8,128)(2,1)S(1)} %get-tuple-element.59), channel_id=1, source_target_pairs={{0,480},{32,0},{64,32},{96,64},{128,96},{160,128},{192,160},{224,1... | collective-permute-start | bytes 245768 | tf_op jit(solution)/shard_map/gather_sequence/ppermute | solution.py:30
  57.4 9.5 %collective-permute-start.10 = (bf16[128,320]{0,1:T(8,128)(2,1)S(1)}, bf16[128,320]{0,1:T(8,128)(2,1)S(1)}, u32[]{:S(2)}, u32[]{:S(2)}) collective-permute-start(bf16[128,320]{0,1:T(8,128)(2,1)S(1)} %get-tuple-element.59), channel_id=1, source_target_pairs={{0,32},{32,64},{64,96},{96,128},{128,160},{160,192},{192,224},{224... | collective-permute-start | bytes 245768 | tf_op jit(solution)/shard_map/gather_sequence/ppermute | solution.py:30
  61.3 9.6 %collective-permute-start.4 = (bf16[128,320]{0,1:T(8,128)(2,1)S(1)}, bf16[128,320]{0,1:T(8,128)(2,1)S(1)}, u32[]{:S(2)}, u32[]{:S(2)}) collective-permute-start(bf16[128,320]{0,1:T(8,128)(2,1)S(1)} %collective-permute-done.3), channel_id=1, source_target_pairs={{0,480},{32,0},{64,32},{96,64},{128,96},{160,128},{192,160},{224,1... | collective-permute-start | bytes 245768 | tf_op jit(solution)/shard_map/gather_sequence/ppermute | solution.py:30
  66.9 9.9 %collective-permute-start.11 = (bf16[128,320]{0,1:T(8,128)(2,1)S(1)}, bf16[128,320]{0,1:T(8,128)(2,1)S(1)}, u32[]{:S(2)}, u32[]{:S(2)}) collective-permute-start(bf16[128,320]{0,1:T(8,128)(2,1)S(1)} %collective-permute-done.10), channel_id=1, source_target_pairs={{0,32},{32,64},{64,96},{96,128},{128,160},{160,192},{192,224},{224... | collective-permute-start | bytes 245768 | tf_op jit(solution)/shard_map/gather_sequence/ppermute | solution.py:30
  70.9 9.7 %collective-permute-start.5 = (bf16[128,320]{0,1:T(8,128)(2,1)S(1)}, bf16[128,320]{0,1:T(8,128)(2,1)S(1)}, u32[]{:S(2)}, u32[]{:S(2)}) collective-permute-start(bf16[128,320]{0,1:T(8,128)(2,1)S(1)} %collective-permute-done.4), channel_id=1, source_target_pairs={{0,480},{32,0},{64,32},{96,64},{128,96},{160,128},{192,160},{224,1... | collective-permute-start | bytes 245768 | tf_op jit(solution)/shard_map/gather_sequence/ppermute | solution.py:30
  76.8 9.4 %collective-permute-start.12 = (bf16[128,320]{0,1:T(8,128)(2,1)S(1)}, bf16[128,320]{0,1:T(8,128)(2,1)S(1)}, u32[]{:S(2)}, u32[]{:S(2)}) collective-permute-start(bf16[128,320]{0,1:T(8,128)(2,1)S(1)} %collective-permute-done.11), channel_id=1, source_target_pairs={{0,32},{32,64},{64,96},{96,128},{128,160},{160,192},{192,224},{224... | collective-permute-start | bytes 245768 | tf_op jit(solution)/shard_map/gather_sequence/ppermute | solution.py:30
  80.6 9.1 %collective-permute-start.6 = (bf16[128,320]{0,1:T(8,128)(2,1)S(1)}, bf16[128,320]{0,1:T(8,128)(2,1)S(1)}, u32[]{:S(2)}, u32[]{:S(2)}) collective-permute-start(bf16[128,320]{0,1:T(8,128)(2,1)S(1)} %collective-permute-done.5), channel_id=1, source_target_pairs={{0,480},{32,0},{64,32},{96,64},{128,96},{160,128},{192,160},{224,1... | collective-permute-start | bytes 245768 | tf_op jit(solution)/shard_map/gather_sequence/ppermute | solution.py:30
  86.2 9.2 %collective-permute-start.13 = (bf16[128,320]{0,1:T(8,128)(2,1)S(1)}, bf16[128,320]{0,1:T(8,128)(2,1)S(1)}, u32[]{:S(2)}, u32[]{:S(2)}) collective-permute-start(bf16[128,320]{0,1:T(8,128)(2,1)S(1)} %collective-permute-done.12), channel_id=1, source_target_pairs={{0,32},{32,64},{64,96},{96,128},{128,160},{160,192},{192,224},{224... | collective-permute-start | bytes 245768 | tf_op jit(solution)/shard_map/gather_sequence/ppermute | solution.py:30
  89.7 8.9 %collective-permute-start.7 = (bf16[128,320]{0,1:T(8,128)(2,1)S(1)}, bf16[128,320]{0,1:T(8,128)(2,1)S(1)}, u32[]{:S(2)}, u32[]{:S(2)}) collective-permute-start(bf16[128,320]{0,1:T(8,128)(2,1)S(1)} %collective-permute-done.6), channel_id=1, source_target_pairs={{0,480},{32,0},{64,32},{96,64},{128,96},{160,128},{192,160},{224,1... | collective-permute-start | bytes 245768 | tf_op jit(solution)/shard_map/gather_sequence/ppermute | solution.py:30
  95.4 9.1 %collective-permute-start.14 = (bf16[128,320]{0,1:T(8,128)(2,1)S(1)}, bf16[128,320]{0,1:T(8,128)(2,1)S(1)}, u32[]{:S(2)}, u32[]{:S(2)}) collective-permute-start(bf16[128,320]{0,1:T(8,128)(2,1)S(1)} %collective-permute-done.13), channel_id=1, source_target_pairs={{0,32},{32,64},{64,96},{96,128},{128,160},{160,192},{192,224},{224... | collective-permute-start | bytes 245768 | tf_op jit(solution)/shard_map/gather_sequence/ppermute | solution.py:30
  98.6 9.0 %collective-permute-start.8 = (bf16[128,320]{0,1:T(8,128)(2,1)S(1)}, bf16[128,320]{0,1:T(8,128)(2,1)S(1)}, u32[]{:S(2)}, u32[]{:S(2)}) collective-permute-start(bf16[128,320]{0,1:T(8,128)(2,1)S(1)} %collective-permute-done.7), channel_id=1, source_target_pairs={{0,480},{32,0},{64,32},{96,64},{128,96},{160,128},{192,160},{224,1... | collective-permute-start | bytes 245768 | tf_op jit(solution)/shard_map/gather_sequence/ppermute | solution.py:30
  104.5 9.0 %collective-permute-start.15 = (bf16[128,320]{0,1:T(8,128)(2,1)S(1)}, bf16[128,320]{0,1:T(8,128)(2,1)S(1)}, u32[]{:S(2)}, u32[]{:S(2)}) collective-permute-start(bf16[128,320]{0,1:T(8,128)(2,1)S(1)} %collective-permute-done.14), channel_id=1, source_target_pairs={{0,32},{32,64},{64,96},{96,128},{128,160},{160,192},{192,224},{224... | collective-permute-start | bytes 245768 | tf_op jit(solution)/shard_map/gather_sequence/ppermute | solution.py:30
  107.6 16.8 %collective-permute-start.9 = (bf16[128,320]{0,1:T(8,128)(2,1)S(1)}, bf16[128,320]{0,1:T(8,128)(2,1)S(1)}, u32[]{:S(2)}, u32[]{:S(2)}) collective-permute-start(bf16[128,320]{0,1:T(8,128)(2,1)S(1)} %collective-permute-done.8), channel_id=1, source_target_pairs={{0,480},{32,0},{64,32},{96,64},{128,96},{160,128},{192,160},{224,1... | collective-permute-start | bytes 245768 | tf_op jit(solution)/shard_map/gather_sequence/ppermute | solution.py:30
  113.6 8.9 %collective-permute-start.16 = (bf16[128,320]{0,1:T(8,128)(2,1)S(1)}, bf16[128,320]{0,1:T(8,128)(2,1)S(1)}, u32[]{:S(2)}, u32[]{:S(2)}) collective-permute-start(bf16[128,320]{0,1:T(8,128)(2,1)S(1)} %collective-permute-done.15), channel_id=1, source_target_pairs={{0,32},{32,64},{64,96},{96,128},{128,160},{160,192},{192,224},{224... | collective-permute-start | bytes 245768 | tf_op jit(solution)/shard_map/gather_sequence/ppermute | solution.py:30
  122.5 7.9 %collective-permute-start.17 = (bf16[128,320]{0,1:T(8,128)(2,1)S(1)}, bf16[128,320]{0,1:T(8,128)(2,1)S(1)}, u32[]{:S(2)}, u32[]{:S(2)}) collective-permute-start(bf16[128,320]{0,1:T(8,128)(2,1)S(1)} %collective-permute-done.16), channel_id=1, source_target_pairs={{0,32},{32,64},{64,96},{96,128},{128,160},{160,192},{192,224},{224... | collective-permute-start | bytes 245768 | tf_op jit(solution)/shard_map/gather_sequence/ppermute | solution.py:30
  135.7 25.0 %collective-permute-start.18 = (bf16[2048,320]{0,1:T(8,128)(2,1)}, bf16[2048,320]{0,1:T(8,128)(2,1)}, u32[]{:S(2)}, u32[]{:S(2)}) collective-permute-start(bf16[2048,320]{0,1:T(8,128)(2,1)} %constant_dynamic-update-slice_fusion.2), channel_id=1, source_target_pairs={{0,8},{8,16},{16,24},{24,0},{1,9},{9,17},{17,25},{25,1},{2,10},{10... | collective-permute-start | bytes 3932168 | tf_op jit(solution)/shard_map/gather_sequence/ppermute | solution.py:30
  138.2 23.5 %collective-permute-start.19 = (bf16[2048,320]{0,1:T(8,128)(2,1)}, bf16[2048,320]{0,1:T(8,128)(2,1)}, u32[]{:S(2)}, u32[]{:S(2)}) collective-permute-start(bf16[2048,320]{0,1:T(8,128)(2,1)} %constant_dynamic-update-slice_fusion.2), channel_id=1, source_target_pairs={{0,24},{8,0},{16,8},{24,16},{1,25},{9,1},{17,9},{25,17},{2,26},{10... | collective-permute-start | bytes 3932168 | tf_op jit(solution)/shard_map/gather_sequence/ppermute | solution.py:30
  157.9 1.7 copy-start.7
  162.3 25.6 %all-to-all-start = ((f32[64,2,2,128]{3,2,1,0:T(2,128)}), f32[64,2,2,128]{3,2,1,0:T(2,128)}, u32[]{:S(2)}, u32[]{:S(2)}) async-start(f32[64,2,2,128]{3,2,1,0:T(2,128)} %broadcast_in_dim.91), calls=%async_computation | async-start | bytes 262144 | tf_op jit(solution)/shard_map/gather_row_stats/all_to_all | solution.py:175
  173.8 24.6 %collective-permute-start.20 = (bf16[1024,320]{0,1:T(8,128)(2,1)}, bf16[1024,320]{0,1:T(8,128)(2,1)}, u32[]{:S(2)}, u32[]{:S(2)}) collective-permute-start(bf16[1024,320]{0,1:T(8,128)(2,1)} %slice.137), channel_id=1, source_target_pairs={{0,8},{8,16},{16,24},{24,0},{1,9},{9,17},{17,25},{25,1},{2,10},{10... | collective-permute-start | bytes 1966088 | tf_op jit(solution)/shard_map/gather_row_stats/ppermute | solution.py:30
  179.2 20.4 %collective-permute-start.21 = (bf16[1024,320]{0,1:T(8,128)(2,1)}, bf16[1024,320]{0,1:T(8,128)(2,1)}, u32[]{:S(2)}, u32[]{:S(2)}) collective-permute-start(bf16[1024,320]{0,1:T(8,128)(2,1)} %slice.138), channel_id=1, source_target_pairs={{0,24},{8,0},{16,8},{24,16},{1,25},{9,1},{17,9},{25,17},{2,26},{10... | collective-permute-start | bytes 1966088 | tf_op jit(solution)/shard_map/gather_row_stats/ppermute | solution.py:30
  191.0 1.8 copy-start.3
  205.9 14.0 %copy-start.11 = (bf16[128,320]{0,1:T(8,128)(2,1)S(1)}, bf16[128,320]{0,1:T(8,128)(2,1)}, u32[]{:S(2)}) copy-start(bf16[128,320]{0,1:T(8,128)(2,1)} %param.11) | copy-start | bytes 245764
  205.9 14.0 %copy-start.12 = (bf16[128,320]{0,1:T(8,128)(2,1)S(1)}, bf16[128,320]{0,1:T(8,128)(2,1)}, u32[]{:S(2)}) copy-start(bf16[128,320]{0,1:T(8,128)(2,1)} %param.12) | copy-start | bytes 245764
  (7 other events, 7.7 us)
Sparse Core Ops, SparseCore 0:
  43.4 89.8 all-gather.1
